TPU v7x, 32 devices: a whole 2x2x4 slice. The times are simulated.
32 devices in a mesh: expert: 16 (over z, y, core), dp: 2 (over x).
Axes of the slice: x: 2, y: 2, z: 4, core: 2. Of those that a mesh axis runs over, the one named last changes fastest.
Arguments:
- tokens: bfloat16 [4096, 2048], P(('expert', 'dp')), may hold values from -6 to 6
- cotangent: bfloat16 [4096, 2048], P(('expert', 'dp')), may hold values from -6 to 6
- expert_ids: int32 [4096, 6], P(('expert', 'dp')), may hold values from 0 to 15, all different within a row; in each aligned block of 128 rows (0 to 127, 128 to 255, ...) at most 60 rows name the same one
- gate_vals: float32 [4096, 6], P(('expert', 'dp')), may hold values from 0.05 to 0.5
- capacity: int32 [16], replicated, may hold values from 384 to 960
- w_gate: bfloat16 [16, 384, 2048], P('expert', 'dp'), may hold values from -0.125 to 0.125
- w_up: bfloat16 [16, 384, 2048], P('expert', 'dp'), may hold values from -0.125 to 0.125
- w_down: bfloat16 [16, 384, 2048], P('expert', 'dp'), may hold values from -0.3125 to 0.3125
Outputs:
- layer_out: bfloat16 [4096, 2048], P(('expert', 'dp'))
- grad_tokens: bfloat16 [4096, 2048], P(('expert', 'dp'))
- grad_gates: float32 [4096, 6], P(('expert', 'dp'))
- grad_gate_w: bfloat16 [16, 384, 2048], P('expert', 'dp')
- grad_up_w: bfloat16 [16, 384, 2048], P('expert', 'dp')
- grad_down_w: bfloat16 [16, 384, 2048], P('expert', 'dp')
Inputs may be any that keep to these rules, and one draw needn't show every extreme that they name: `expert_ids`: within the 128 rows of one device no expert is named more than 60 times, a bound that some block reaches.
All inputs are finite; a program needn't handle non-finite values.
Results may differ from a plain program's by a relative error of at most 0.0065.
Values may be sent and summed in bfloat16 or wider, within the bound.
No kernel may reach another device: no remote copies, remote signals or barrier semaphores. Data moves between devices by JAX's collectives and lax.ppermute only.
A program may use at most 128 MiB of HBM per device.

v0:
```python
import jax
import jax.numpy as jnp
import numpy as np
from jax import lax
from jax.sharding import Mesh
from jax.sharding import PartitionSpec as P


def shifted(value, axis, count, shift):
    return lax.ppermute(value, axis, [(j, (j + shift) % count) for j in range(count)])


def in_three(value):
    first = value.astype(jnp.bfloat16)
    rest = value - first.astype(jnp.float32)
    second = rest.astype(jnp.bfloat16)
    third = (rest - second.astype(jnp.float32)).astype(jnp.bfloat16)
    return jnp.concatenate([first, second, third], axis=0)


def on_device(tokens, cotangent, expert_ids, gate_vals, capacity, w_gate, w_up, w_down):
    tok_rows, width = tokens.shape
    top_count = expert_ids.shape[1]
    experts = capacity.shape[0]
    local_experts, hidden_part, _ = w_gate.shape
    slots = max(2, (5 * tok_rows * top_count + 4 * experts - 1) // (4 * experts))
    n_in = lax.axis_size("inner")
    n_dp = lax.axis_size("dp")
    half = lax.axis_index("half")
    inner = lax.axis_index("inner")
    source = half * n_in + inner
    n_src = 2 * n_in
    half_experts = n_in * local_experts
    half_rows = half_experts * slots
    weights = jnp.concatenate([w_gate, w_up, w_down], axis=0)
    pieces = [weights] + [shifted(weights, "dp", n_dp, d) for d in range(1, n_dp)]
    both_rows = jnp.concatenate([tokens, cotangent], axis=1)
    partner_rows = shifted(both_rows, "half", 2, 1)
    partner_gates = shifted(gate_vals, "half", 2, 1)
    flat_ids = expert_ids.reshape(-1)
    one_hot = (flat_ids[:, None] == jnp.arange(experts, dtype=jnp.int32)[None, :]).astype(jnp.int32)
    running = jnp.cumsum(one_hot, axis=0)
    local_rank = jnp.sum(running * one_hot, axis=1) - 1
    counts = running[-1]
    count_rows = jnp.where(
        jnp.arange(n_src, dtype=jnp.int32)[:, None] == source, counts[None, :], 0
    )
    all_counts = lax.psum(count_rows.astype(jnp.float32), ("half", "inner")).astype(jnp.int32)
    code = (flat_ids * slots + local_rank).reshape(tok_rows, top_count)
    partner_code = shifted(code, "half", 2, 1)
    all_rows = jnp.concatenate([both_rows, partner_rows], axis=0)
    all_gates = jnp.concatenate([gate_vals, partner_gates], axis=0)
    all_code = jnp.concatenate([code, partner_code], axis=0)
    local = all_code // slots - half * half_experts
    inside = (local >= 0) & (local < half_experts)
    side = (jnp.arange(2 * tok_rows, dtype=jnp.int32) >= tok_rows).astype(jnp.int32)[:, None]
    dest = jnp.where(inside, (local * 2 + side) * slots + all_code % slots, 2 * half_rows)
    row_of = jnp.broadcast_to(jnp.arange(2 * tok_rows, dtype=jnp.int32)[:, None], dest.shape)
    filled_by = (
        jnp.full((2 * half_rows,), -1, jnp.int32)
        .at[dest.reshape(-1)]
        .set(row_of.reshape(-1), mode="drop")
    )
    slot_gate = (
        jnp.zeros((2 * half_rows,), jnp.float32)
        .at[dest.reshape(-1)]
        .set(all_gates.reshape(-1), mode="drop")
    )
    pick = (filled_by[:, None] == jnp.arange(2 * tok_rows, dtype=jnp.int32)[None, :]).astype(
        jnp.bfloat16
    )
    picked = jnp.dot(pick, all_rows, preferred_element_type=jnp.float32)
    send_x = picked[:, :width].astype(jnp.bfloat16)
    send_c = (slot_gate[:, None] * picked[:, width:]).astype(jnp.bfloat16)
    send = jnp.concatenate([send_x, send_c], axis=1).reshape(half_experts, 2 * slots, 2 * width)
    got = lax.all_to_all(send, "inner", split_axis=0, concat_axis=0, tiled=True)
    got = got.reshape(n_in, local_experts, 2, slots, 2 * width)
    earlier = jnp.cumsum(all_counts, axis=0) - all_counts
    holders = jnp.arange(n_in, dtype=jnp.int32)[:, None]
    halves = jnp.stack([half, 1 - half])[None, :]
    sources = halves * n_in + holders
    mine = (half * n_in + inner) * local_experts + jnp.arange(local_experts, dtype=jnp.int32)
    before = earlier[sources][:, :, mine].transpose(0, 2, 1)
    ranks = jnp.arange(slots, dtype=jnp.int32)
    keep = before[..., None] + ranks < capacity[mine][None, :, None, None]
    got = jnp.where(keep[..., None], got, jnp.zeros((), got.dtype))
    got = got.transpose(1, 0, 2, 3, 4).reshape(local_experts, n_in * 2 * slots, 2 * width)
    rows_in = got[:, :, :width]
    rows_cot = got[:, :, width:]
    full = jnp.concatenate(pieces, axis=1)
    full_gate = full[:local_experts]
    full_up = full[local_experts : 2 * local_experts]
    full_down = full[2 * local_experts :]
    gate_pre = jnp.einsum("erd,efd->erf", rows_in, full_gate, preferred_element_type=jnp.float32)
    up_pre = jnp.einsum("erd,efd->erf", rows_in, full_up, preferred_element_type=jnp.float32)
    sigmoid_gate = jax.nn.sigmoid(gate_pre)
    activated = gate_pre * sigmoid_gate
    hidden = (activated * up_pre).astype(jnp.bfloat16)
    out_rows = jnp.einsum(
        "erf,efd->erd", hidden, full_down, preferred_element_type=jnp.float32
    ).astype(jnp.bfloat16)
    d_hidden = jnp.einsum("erd,efd->erf", rows_cot, full_down, preferred_element_type=jnp.float32)
    d_gate = (d_hidden * up_pre * (sigmoid_gate + activated * (1.0 - sigmoid_gate))).astype(
        jnp.bfloat16
    )
    d_up = (d_hidden * activated).astype(jnp.bfloat16)
    dx_rows = jnp.einsum("erf,efd->erd", d_gate, full_gate, preferred_element_type=jnp.float32)
    dx_rows = (
        dx_rows + jnp.einsum("erf,efd->erd", d_up, full_up, preferred_element_type=jnp.float32)
    ).astype(jnp.bfloat16)
    part_down = jnp.einsum("erf,erd->efd", hidden, rows_cot, preferred_element_type=jnp.float32)
    part_gate = jnp.einsum("erf,erd->efd", d_gate, rows_in, preferred_element_type=jnp.float32)
    part_up = jnp.einsum("erf,erd->efd", d_up, rows_in, preferred_element_type=jnp.float32)
    out_rows = out_rows.reshape(local_experts, n_in, 2, slots, width)
    dx_rows = dx_rows.reshape(local_experts, n_in, 2, slots, width)

    def returning(which):
        back = jnp.stack([out_rows[:, :, which], dx_rows[:, :, which]], axis=2)
        back = back.transpose(1, 0, 2, 3, 4).reshape(half_experts, 2, slots, width)
        return lax.all_to_all(back, "inner", split_axis=0, concat_axis=0, tiled=True)

    parts = jnp.concatenate([part_gate, part_up, part_down], axis=0)
    summed = parts[:, :hidden_part]
    for d in range(1, n_dp):
        block = parts[:, d * hidden_part : (d + 1) * hidden_part].astype(jnp.bfloat16)
        summed = summed + shifted(block, "dp", n_dp, -d).astype(jnp.float32)
    summed = summed.astype(jnp.bfloat16)
    grad_gate_w = summed[:local_experts]
    grad_up_w = summed[local_experts : 2 * local_experts]
    grad_down_w = summed[2 * local_experts :]
    place = jnp.where(inside, local * slots + all_code % slots, half_rows)
    columns = jnp.arange(half_rows, dtype=jnp.int32)

    def combine(which):
        back = returning(which)
        out_part = back[:, 0].reshape(half_rows, width)
        dx_part = back[:, 1].reshape(half_rows, width)
        rows = slice(which * tok_rows, (which + 1) * tok_rows)
        hit = place[rows][:, :, None] == columns[None, None, :]
        weight = jnp.sum(jnp.where(hit, all_gates[rows][:, :, None], 0.0), axis=1)
        ones = jnp.sum(hit.astype(jnp.float32), axis=1).astype(jnp.bfloat16)
        layer = jnp.dot(in_three(weight), out_part, preferred_element_type=jnp.float32)
        layer = layer[:tok_rows] + layer[tok_rows : 2 * tok_rows] + layer[2 * tok_rows :]
        grads = jnp.dot(ones, dx_part, preferred_element_type=jnp.float32)
        scores = jnp.dot(all_rows[rows, width:], out_part.T, preferred_element_type=jnp.float32)
        gg = jnp.sum(jnp.where(hit, scores[:, None, :], 0.0), axis=2)
        return (layer, grads, gg)

    partner_layer, partner_grads, partner_gg = combine(1)
    returned = shifted(
        jnp.concatenate([partner_layer, partner_grads], axis=1).astype(jnp.bfloat16), "half", 2, 1
    )
    returned_gg = shifted(partner_gg, "half", 2, 1)
    own_layer, own_grads, own_gg = combine(0)
    layer_out = (own_layer + returned[:, :width].astype(jnp.float32)).astype(jnp.bfloat16)
    grad_tokens = (own_grads + returned[:, width:].astype(jnp.float32)).astype(jnp.bfloat16)
    grad_gates = own_gg + returned_gg
    return (layer_out, grad_tokens, grad_gates, grad_gate_w, grad_up_w, grad_down_w)


def solution(mesh):
    n_expert = mesh.shape["expert"]
    n_dp = mesh.shape["dp"]
    devices = np.asarray(mesh.devices).reshape(2, n_expert // 2, n_dp)
    split = Mesh(devices, ("half", "inner", "dp"))
    rows = P(("half", "inner", "dp"), None)
    weights = P(("half", "inner"), "dp", None)
    return jax.shard_map(
        on_device,
        mesh=split,
        in_specs=(rows, rows, rows, rows, P(), weights, weights, weights),
        out_specs=(rows, rows, rows, weights, weights, weights),
        check_vma=False,
    )
```

profile of v0, /device:TPU:0, one launch (start us, length us, event | category | flops | bytes accessed | tf_op | source)
XLA Modules:
  0.0 487.5 jit_solution(17768026236895901356)
XLA Ops:
  2.8 4.1 collective-permute-start.1
  7.9 1.7 reduce-window.6
  10.4 2.9 collective-permute-start.2
  13.7 39.1 %collective-permute-done = s32[128,6]{0,1:T(8,128)S(1)} collective-permute-done((s32[128,6]{0,1:T(8,128)S(1)}, s32[128,6]{0,1:T(8,128)S(1)}, u32[]{:S(2)}, u32[]{:S(2)}) %collective-permute-start) | collective-permute-done | bytes 3104 | tf_op jit(solution)/shard_map/ppermute | solution.py:10
  54.2 6.2 %scatter_custom_fusion = s32[960]{0:T(1024)S(1)} fusion(s32[1536]{0:T(1024)S(1)} %fusion.47, s32[1536]{0:T(1024)S(1)} %reshape.415, s32[]{:T(128)} %constant.25.clone.1), kind=kCustom, calls=%fused_computation.128 | custom fusion | bytes 3844 | tf_op jit(solution)/shard_map/scatter | solution.py:62
  60.4 6.2 %scatter_custom_fusion.1 = f32[960]{0:T(1024)S(1)} fusion(s32[1536]{0:T(1024)S(1)} %fusion.47, f32[1536]{0:T(1024)S(1)} %reshape.423, f32[]{:T(128)} %constant.34.clone.1), kind=kCustom, calls=%fused_computation.126 | custom fusion | bytes 3844 | tf_op jit(solution)/shard_map/scatter | solution.py:67
  66.6 2.2 fusion.7
  68.8 2.6 slice.256
  71.4 2.5 fusion
  73.9 7.4 %pad_maximum_fusion.1 = bf16[960,4096]{1,0:T(8,128)(2,1)} fusion(bf16[960,2048]{1,0:T(8,128)(2,1)} %fusion, bf16[960,2048]{1,0:T(8,128)(2,1)} %slice.256), kind=kLoop, calls=%fused_computation.7 | loop fusion | flops 15728640 | bytes 15728640 | tf_op jit(solution)/shard_map/concatenate | solution.py:75
  81.3 5.1 %all-to-all-start = ((bf16[8,120,4096]{2,1,0:T(8,128)(2,1)}), bf16[8,120,4096]{2,1,0:T(8,128)(2,1)}, u32[]{:S(2)}, u32[]{:S(2)}) async-start(bf16[8,120,4096]{2,1,0:T(8,128)(2,1)} %bitcast.83), calls=%async_computation | async-start | bytes 15728640 | tf_op jit(solution)/shard_map/all_to_all | solution.py:76
  87.9 1.6 collective-permute-start.3
  89.8 109.6 %psum.7 = f32[16,16]{1,0:T(8,128)S(1)} all-reduce(f32[16,16]{1,0:T(8,128)S(1)} %select_convert_fusion), channel_id=1, replica_groups=mesh['half'=2,'inner'=8,'dp'=2] {'half','inner'}, use_global_device_ids=true, to_apply=%region_4.5 | all-reduce | flops 256 | bytes 2048 | tf_op jit(solution)/shard_map/psum | solution.py:48
  201.9 6.9 %bitcast_select_fusion = bf16[1,960,4096]{2,1,0:T(8,128)(2,1)} fusion(pred[960]{0:T(1024)(128)(4,1)S(1)} %lt.80, bf16[1,960,4096]{2,1,0:T(8,128)(2,1)} %bitcast.81), kind=kLoop, calls=%fused_computation.8 | loop fusion | flops 3932160 | bytes 15729600 | tf_op jit(solution)/shard_map/jit(_where)/select_n | solution.py:86
  208.8 4.7 fusion.3
  213.5 3.3 fusion.6
  216.9 4.7 multiply_convert_fusion.2
  221.5 3.6 fusion.61
  225.1 5.3 %add_convert_fusion = bf16[960,2048]{1,0:T(8,128)(2,1)} fusion(f32[960,2048]{1,0:T(8,128)S(1)} %fusion.61, bf16[960,384]{1,0:T(8,128)(2,1)S(1)} %get-tuple-element.45, bf16[3,192,2048]{2,1,0:T(8,128)(2,1)S(1)} %constant_dynamic-update-slice_fusion.2, bf16[3,192,2048]{2,1,0:T(8,128)(2,1)} %collective-permute-done.3), kind=kOutput, calls=%fused_computation.9 | convolution fusion | flops 1517027328 | bytes 17252352 | tf_op jit(solution)/shard_map/erf,efd->erd/dot_general | solution.py:107
  230.4 5.1 %reshape.356 = bf16[1,8,2,60,2048]{4,3,2,1,0:T(8,128)(2,1)} reshape(bf16[960,2048]{1,0:T(8,128)(2,1)} %add_convert_fusion) | data formatting | bytes 7864320 | tf_op jit(solution)/shard_map/reshape | solution.py:115
  235.5 5.4 %convolution_convert_fusion = bf16[960,2048]{1,0:T(8,128)(2,1)} fusion(bf16[960,384]{1,0:T(8,128)(2,1)} %get-tuple-element.44, bf16[3,192,2048]{2,1,0:T(8,128)(2,1)} %collective-permute-done.3, bf16[3,192,2048]{2,1,0:T(8,128)(2,1)S(1)} %constant_dynamic-update-slice_fusion.2), kind=kOutput, calls=%fused_computation.25 | convolution fusion | flops 1515061248 | bytes 9388032 | tf_op jit(solution)/shard_map/erf,efd->erd/dot_general | solution.py:99
  240.9 4.9 %reshape.354 = bf16[1,8,2,60,2048]{4,3,2,1,0:T(8,128)(2,1)} reshape(bf16[960,2048]{1,0:T(8,128)(2,1)} %convolution_convert_fusion) | data formatting | bytes 7864320 | tf_op jit(solution)/shard_map/reshape | solution.py:114
  245.8 4.8 fusion.64
  251.0 6.0 %copy.93 = bf16[8,2,60,2048]{3,1,2,0:T(2,128)(2,1)} copy(bf16[8,2,60,2048]{3,2,1,0:T(8,128)(2,1)S(1)} %maximum_bitcast_fusion.1) | data formatting | bytes 7864320 | tf_op jit(solution)/shard_map/reshape;transpose | solution.py:119
  257.1 4.5 all-to-all-start.2
  261.6 2.0 maximum_bitcast_fusion
  263.6 6.0 %copy.92 = bf16[8,2,60,2048]{3,1,2,0:T(2,128)(2,1)} copy(bf16[8,2,60,2048]{3,2,1,0:T(8,128)(2,1)S(1)} %maximum_bitcast_fusion) | data formatting | bytes 7864320 | tf_op jit(solution)/shard_map/reshape;transpose | solution.py:119
  269.6 37.3 %all-to-all-done.2 = bf16[8,2,60,2048]{3,1,2,0:T(2,128)(2,1)} async-done(((bf16[8,2,60,2048]{3,1,2,0:T(2,128)(2,1)}), bf16[8,2,60,2048]{3,1,2,0:T(2,128)(2,1)}, u32[]{:S(2)}, u32[]{:S(2)}) %all-to-all-start.2) | async-done | bytes 3932192 | tf_op jit(solution)/shard_map/all_to_all | solution.py:120
  306.9 4.9 %all-to-all-start.1 = ((bf16[8,2,60,2048]{3,1,2,0:T(2,128)(2,1)}), bf16[8,2,60,2048]{3,1,2,0:T(2,128)(2,1)}, u32[]{:S(2)}, u32[]{:S(2)}) async-start(bf16[8,2,60,2048]{3,1,2,0:T(2,128)(2,1)} %copy.92), calls=%async_computation.1 | async-start | bytes 7864320 | tf_op jit(solution)/shard_map/all_to_all | solution.py:120
  311.9 4.1 convolution_bitcast_fusion
  316.0 4.1 convolution_bitcast_fusion.1
  320.2 1.8 fusion.4
  323.6 1.6 collective-permute-start.6
  325.2 52.1 %collective-permute-done.6 = bf16[3,192,2048]{2,1,0:T(8,128)(2,1)S(1)} collective-permute-done((bf16[3,192,2048]{2,1,0:T(8,128)(2,1)S(1)}, bf16[3,192,2048]{2,1,0:T(8,128)(2,1)S(1)}, u32[]{:S(2)}, u32[]{:S(2)}) %collective-permute-start.6) | collective-permute-done | bytes 2359328 | tf_op jit(solution)/shard_map/ppermute | solution.py:10
  378.1 1.4 fusion.66
  379.6 20.6 %slice_reduce_fusion.2 = (bf16[8,60,2048]{2,1,0:T(8,128)(2,1)}, bf16[8,60,2048]{2,1,0:T(8,128)(2,1)}) fusion(bf16[8,2,60,2048]{3,1,2,0:T(2,128)(2,1)} %all-to-all-done.2), kind=kLoop, calls=%fused_computation.21 | loop fusion | bytes 7864320 | tf_op jit(solution)/shard_map/slice | solution.py:136
  400.2 1.8 reshape_squeeze.13
  403.3 20.7 %slice_reduce_fusion = (bf16[8,60,2048]{2,1,0:T(8,128)(2,1)}, bf16[8,60,2048]{2,1,0:T(8,128)(2,1)}) fusion(bf16[8,2,60,2048]{3,1,2,0:T(2,128)(2,1)} %all-to-all-done.1), kind=kLoop, calls=%fused_computation.19 | loop fusion | bytes 7864320 | tf_op jit(solution)/shard_map/slice | solution.py:137
  424.0 1.7 reshape_squeeze.12
  425.8 2.5 fusion.29
  428.5 2.7 reshape_squeeze.14
  431.2 2.1 convolution_convert_fusion.1
  434.4 2.9 collective-permute-start.4
  438.6 2.7 fusion.23
  441.2 2.9 reshape_squeeze.15
  444.7 38.1 %collective-permute-done.4 = bf16[128,4096]{1,0:T(8,128)(2,1)} collective-permute-done((bf16[128,4096]{1,0:T(8,128)(2,1)}, bf16[128,4096]{1,0:T(8,128)(2,1)}, u32[]{:S(2)}, u32[]{:S(2)}) %collective-permute-start.4) | collective-permute-done | bytes 1048608 | tf_op jit(solution)/shard_map/ppermute | solution.py:10
  482.9 2.1 fusion.19
  485.0 2.3 add_convert_fusion.1
  (107 shorter events, 16.9 us)
Async XLA Ops:
  0.6 9.7 %copy-start.12 = (s32[128,6]{0,1:T(8,128)S(1)}, s32[128,6]{0,1:T(8,128)}, u32[]{:S(2)}) copy-start(s32[128,6]{0,1:T(8,128)} %param.10) | copy-start | bytes 9220
  0.6 9.8 %copy-start.11 = (f32[128,6]{0,1:T(8,128)S(1)}, f32[128,6]{0,1:T(8,128)}, u32[]{:S(2)}) copy-start(f32[128,6]{0,1:T(8,128)} %param.11) | copy-start | bytes 9220
  2.8 63.7 %collective-permute-start.1 = (bf16[128,4096]{1,0:T(8,128)(2,1)S(1)}, bf16[128,4096]{1,0:T(8,128)(2,1)S(1)}, u32[]{:S(2)}, u32[]{:S(2)}) collective-permute-start(bf16[128,4096]{1,0:T(8,128)(2,1)S(1)} %constant_dynamic-update-slice_fusion), channel_id=1, source_target_pairs={{0,16},{16,0},{1,17},{17,1},{2,18},{18,2},{3,19},{19,3},{4,20},{20... | collective-permute-start | bytes 3145736 | tf_op jit(solution)/shard_map/ppermute | solution.py:10
  10.3 42.5 %collective-permute-start = (s32[128,6]{0,1:T(8,128)S(1)}, s32[128,6]{0,1:T(8,128)S(1)}, u32[]{:S(2)}, u32[]{:S(2)}) collective-permute-start(s32[128,6]{0,1:T(8,128)S(1)} %multiply_add_fusion), channel_id=1, source_target_pairs={{0,16},{16,0},{1,17},{17,1},{2,18},{18,2},{3,19},{19,3},{4,20},{20... | collective-permute-start | bytes 9224 | tf_op jit(solution)/shard_map/ppermute | solution.py:10
  10.4 43.4 %collective-permute-start.2 = (f32[128,6]{0,1:T(8,128)S(1)}, f32[128,6]{0,1:T(8,128)S(1)}, u32[]{:S(2)}, u32[]{:S(2)}) collective-permute-start(f32[128,6]{0,1:T(8,128)S(1)} %copy-done.11), channel_id=1, source_target_pairs={{0,16},{16,0},{1,17},{17,1},{2,18},{18,2},{3,19},{19,3},{4,20},{20... | collective-permute-start | bytes 9224 | tf_op jit(solution)/shard_map/ppermute | solution.py:10
  66.6 2.3 copy-start.4
  81.3 5.1 %copy-start.7 = (bf16[1,192,2048]{2,1,0:T(8,128)(2,1)S(1)}, bf16[1,192,2048]{2,1,0:T(8,128)(2,1)}, u32[]{:S(2)}) copy-start(bf16[1,192,2048]{2,1,0:T(8,128)(2,1)} %param.13) | copy-start | bytes 2359300
  81.3 120.6 %all-to-all-start = ((bf16[8,120,4096]{2,1,0:T(8,128)(2,1)}), bf16[8,120,4096]{2,1,0:T(8,128)(2,1)}, u32[]{:S(2)}, u32[]{:S(2)}) async-start(bf16[8,120,4096]{2,1,0:T(8,128)(2,1)} %bitcast.83), calls=%async_computation | async-start | bytes 15728640 | tf_op jit(solution)/shard_map/all_to_all | solution.py:76
  86.4 1.4 copy-start.8
  86.4 114.0 %copy-start.13 = (s32[16]{0:T(128)S(1)}, s32[16]{0:T(128)}, u32[]{:S(2)}) copy-start(s32[16]{0:T(128)} %param.12) | copy-start | bytes 196
  87.9 121.0 %collective-permute-start.3 = (bf16[3,192,2048]{2,1,0:T(8,128)(2,1)S(1)}, bf16[3,192,2048]{2,1,0:T(8,128)(2,1)}, u32[]{:S(2)}, u32[]{:S(2)}) collective-permute-start(bf16[3,192,2048]{2,1,0:T(8,128)(2,1)S(1)} %constant_dynamic-update-slice_fusion.2), channel_id=1, source_target_pairs={{0,1},{1,0},{2,3},{3,2},{4,5},{5,4},{6,7},{7,6},{8,9},{9,8},{10,11... | collective-permute-start | bytes 7077896 | tf_op jit(solution)/shard_map/ppermute | solution.py:10
  208.8 4.7 copy-start.2
  221.5 3.6 copy-start.9
  257.1 49.9 %all-to-all-start.2 = ((bf16[8,2,60,2048]{3,1,2,0:T(2,128)(2,1)}), bf16[8,2,60,2048]{3,1,2,0:T(2,128)(2,1)}, u32[]{:S(2)}, u32[]{:S(2)}) async-start(bf16[8,2,60,2048]{3,1,2,0:T(2,128)(2,1)} %copy.93), calls=%async_computation.2 | async-start | bytes 7864320 | tf_op jit(solution)/shard_map/all_to_all | solution.py:120
  306.9 96.3 %all-to-all-start.1 = ((bf16[8,2,60,2048]{3,1,2,0:T(2,128)(2,1)}), bf16[8,2,60,2048]{3,1,2,0:T(2,128)(2,1)}, u32[]{:S(2)}, u32[]{:S(2)}) async-start(bf16[8,2,60,2048]{3,1,2,0:T(2,128)(2,1)} %copy.92), calls=%async_computation.1 | async-start | bytes 7864320 | tf_op jit(solution)/shard_map/all_to_all | solution.py:120
  311.9 4.1 copy-start.10
  311.9 8.3 %slice-start = ((s8[7864320]{0:T(1024)(128)(4,1)}), s8[4194304]{0:T(1024)(128)(4,1)S(1)}, s32[]{:S(2)}) async-start(s8[7864320]{0:T(1024)(128)(4,1)} %bitcast.84), calls=%async_computation.3 | async-start | bytes 8388608
  316.0 4.2 slice-start.1
  316.0 4.2 copy-start.14
  323.6 53.7 %collective-permute-start.6 = (bf16[3,192,2048]{2,1,0:T(8,128)(2,1)S(1)}, bf16[3,192,2048]{2,1,0:T(8,128)(2,1)S(1)}, u32[]{:S(2)}, u32[]{:S(2)}) collective-permute-start(bf16[3,192,2048]{2,1,0:T(8,128)(2,1)S(1)} %slice.257), channel_id=1, source_target_pairs={{0,1},{1,0},{2,3},{3,2},{4,5},{5,4},{6,7},{7,6},{8,9},{9,8},{10,11... | collective-permute-start | bytes 7077896 | tf_op jit(solution)/shard_map/ppermute | solution.py:10
  400.2 1.9 copy-start.5
  402.0 21.9 %copy-start = (bf16[480,2048]{1,0:T(8,128)(2,1)}, bf16[480,2048]{1,0:T(8,128)(2,1)S(1)}, u32[]{:S(2)}) copy-start(bf16[480,2048]{1,0:T(8,128)(2,1)S(1)} %reshape_squeeze.13) | copy-start | bytes 5898244
  403.2 41.0 %collective-permute-start.5 = (f32[128,6]{0,1:T(8,128)S(1)}, f32[128,6]{0,1:T(8,128)S(1)}, u32[]{:S(2)}, u32[]{:S(2)}) collective-permute-start(f32[128,6]{0,1:T(8,128)S(1)} %get-tuple-element.32), channel_id=1, source_target_pairs={{0,16},{16,0},{1,17},{17,1},{2,18},{18,2},{3,19},{19,3},{4,20},{20... | collective-permute-start | bytes 9224 | tf_op jit(solution)/shard_map/ppermute | solution.py:10
  431.2 6.1 %copy-start.6 = (bf16[128,2048]{1,0:T(8,128)(2,1)S(1)}, bf16[128,2048]{1,0:T(8,128)(2,1)}, u32[]{:S(2)}) copy-start(bf16[128,2048]{1,0:T(8,128)(2,1)} %param.9) | copy-start | bytes 1572868
  434.4 48.4 %collective-permute-start.4 = (bf16[128,4096]{1,0:T(8,128)(2,1)}, bf16[128,4096]{1,0:T(8,128)(2,1)}, u32[]{:S(2)}, u32[]{:S(2)}) collective-permute-start(bf16[128,4096]{1,0:T(8,128)(2,1)} %pad_maximum_fusion.3), channel_id=1, source_target_pairs={{0,16},{16,0},{1,17},{17,1},{2,18},{18,2},{3,19},{19,3},{4,20},{20... | collective-permute-start | bytes 3145736 | tf_op jit(solution)/shard_map/ppermute | solution.py:10
  441.2 41.6 %copy-start.1 = (f32[384,2048]{1,0:T(8,128)S(1)}, f32[384,2048]{1,0:T(8,128)}, u32[]{:S(2)}) copy-start(f32[384,2048]{1,0:T(8,128)} %fusion.23) | copy-start | bytes 9437188
  444.1 40.9 %copy-start.3 = (bf16[480,2048]{1,0:T(8,128)(2,1)S(1)}, bf16[480,2048]{1,0:T(8,128)(2,1)}, u32[]{:S(2)}) copy-start(bf16[480,2048]{1,0:T(8,128)(2,1)} %reshape_squeeze.15) | copy-start | bytes 5898244
where the time goes:
time: 495 us; the launch traced here: 487 us
  waiting for transfers between devices  167 us (34%)
  blocking collectives  110 us (22%)
  local copies, waits for them, and re-layouts  103 us (21%)
  matrix products  50.3 us (10%)
  other arithmetic  29.1 us (6%)
  starting transfers between devices  27.9 us (6%)
    ppermute x7, waiting for transfers between devices, shifted(): lax.ppermute(value, axis, [(j, (j + shift) % count) for j in range(count)])  129 us
    psum x1, blocking collectives, on_device(): lax.psum(count_rows.astype(jnp.float32), ('half', 'inner'))  110 us
    all_to_all x2, waiting for transfers between devices, returning(): lax.all_to_all(back, 'inner', split_axis=0, concat_axis=0, tiled=True)  37.3 us
    slice x1, local copies, waits for them, and re-layouts, combine(): dx_part = back[:, 1].reshape(half_rows, width)  20.7 us
    slice x1, local copies, waits for them, and re-layouts, combine(): out_part = back[:, 0].reshape(half_rows, width)  20.6 us
    ppermute x7, starting transfers between devices, shifted(): lax.ppermute(value, axis, [(j, (j + shift) % count) for j in range(count)])  13.3 us
    another operation x2, local copies, waits for them, and re-layouts, returning(): back = back.transpose(1, 0, 2, 3, 4).reshape(half_experts, 2, slots, width)  12.1 us
  transfers between devices with their start and end apart: 10, of which 4 were waited for; matrix products, arithmetic and copies ran while one was open for 23% of the time, Pallas kernels for 0%

commit v1 on v0

--- a/solution.py
+++ b/solution.py
@@ -4,6 +4,11 @@
 from jax import lax
 from jax.sharding import Mesh
 from jax.sharding import PartitionSpec as P
+
+
+def by_each_axis(value_2, axis_one, axis_two):
+    partial = lax.psum(value_2, axis_one)
+    return lax.psum(partial, axis_two)
 
 
 def shifted(value, axis, count, shift):
@@ -45,7 +50,7 @@
     count_rows = jnp.where(
         jnp.arange(n_src, dtype=jnp.int32)[:, None] == source, counts[None, :], 0
     )
-    all_counts = lax.psum(count_rows.astype(jnp.float32), ("half", "inner")).astype(jnp.int32)
+    all_counts = by_each_axis(count_rows.astype(jnp.float32), "inner", "half").astype(jnp.int32)
     code = (flat_ids * slots + local_rank).reshape(tok_rows, top_count)
     partner_code = shifted(code, "half", 2, 1)
     all_rows = jnp.concatenate([both_rows, partner_rows], axis=0)

time: 495 us -> 484 us (0.978)
  blocking collectives: 110 us -> 97.7 us
    psum x1 -> x2, blocking collectives: 110 us -> 97.7 us  [the longest x1 91.6 us: by_each_axis(): partial = lax.psum(value_2, axis_one)]
  transfers between devices with their start and end apart: 10 -> 10, of which waited for: 4 -> 4; matrix products, arithmetic and copies ran while one was open for 23% -> 24% of each run, Pallas kernels for 0% -> 0%
where the time goes in v1:
time: 484 us; the launch traced here: 477 us
  waiting for transfers between devices  168 us (35%)
  local copies, waits for them, and re-layouts  103 us (21%)
  blocking collectives  97.7 us (20%)
  matrix products  50.3 us (10%)
  other arithmetic  29.1 us (6%)
  starting transfers between devices  27.9 us (6%)
    ppermute x7, waiting for transfers between devices, shifted(): lax.ppermute(value, axis, [(j, (j + shift) % count) for j in range(count)])  130 us
    psum x1, blocking collectives, by_each_axis(): partial = lax.psum(value_2, axis_one)  91.6 us
    all_to_all x2, waiting for transfers between devices, returning(): lax.all_to_all(back, 'inner', split_axis=0, concat_axis=0, tiled=True)  37.3 us
    slice x1, local copies, waits for them, and re-layouts, combine(): dx_part = back[:, 1].reshape(half_rows, width)  20.7 us
    slice x1, local copies, waits for them, and re-layouts, combine(): out_part = back[:, 0].reshape(half_rows, width)  20.6 us
    ppermute x7, starting transfers between devices, shifted(): lax.ppermute(value, axis, [(j, (j + shift) % count) for j in range(count)])  13.3 us
    another operation x2, local copies, waits for them, and re-layouts, returning(): back = back.transpose(1, 0, 2, 3, 4).reshape(half_experts, 2, slots, width)  12.1 us
  transfers between devices with their start and end apart: 10, of which 4 were waited for; matrix products, arithmetic and copies ran while one was open for 24% of the time, Pallas kernels for 0%

profile of v1, /device:TPU:0, one launch (start us, length us, event | category | flops | bytes accessed | tf_op | source)
XLA Modules:
  0.0 476.7 jit_solution(10421052450713779993)
XLA Ops:
  2.8 4.1 collective-permute-start.1
  7.9 1.7 reduce-window.6
  10.4 2.9 collective-permute-start.2
  13.7 39.1 %collective-permute-done = s32[128,6]{0,1:T(8,128)S(1)} collective-permute-done((s32[128,6]{0,1:T(8,128)S(1)}, s32[128,6]{0,1:T(8,128)S(1)}, u32[]{:S(2)}, u32[]{:S(2)}) %collective-permute-start) | collective-permute-done | bytes 3104 | tf_op jit(solution)/shard_map/ppermute | solution.py:15
  54.2 6.2 %scatter_custom_fusion = s32[960]{0:T(1024)S(1)} fusion(s32[1536]{0:T(1024)S(1)} %fusion.47, s32[1536]{0:T(1024)S(1)} %reshape.415, s32[]{:T(128)} %constant.25.clone.1), kind=kCustom, calls=%fused_computation.128 | custom fusion | bytes 3844 | tf_op jit(solution)/shard_map/scatter | solution.py:67
  60.4 6.2 %scatter_custom_fusion.1 = f32[960]{0:T(1024)S(1)} fusion(s32[1536]{0:T(1024)S(1)} %fusion.47, f32[1536]{0:T(1024)S(1)} %reshape.423, f32[]{:T(128)} %constant.34.clone.1), kind=kCustom, calls=%fused_computation.126 | custom fusion | bytes 3844 | tf_op jit(solution)/shard_map/scatter | solution.py:72
  66.6 2.2 fusion.7
  68.8 2.6 slice.256
  71.4 2.5 fusion
  73.9 7.4 %pad_maximum_fusion.1 = bf16[960,4096]{1,0:T(8,128)(2,1)} fusion(bf16[960,2048]{1,0:T(8,128)(2,1)} %fusion, bf16[960,2048]{1,0:T(8,128)(2,1)} %slice.256), kind=kLoop, calls=%fused_computation.7 | loop fusion | flops 15728640 | bytes 15728640 | tf_op jit(solution)/shard_map/concatenate | solution.py:80
  81.3 5.1 %all-to-all-start = ((bf16[8,120,4096]{2,1,0:T(8,128)(2,1)}), bf16[8,120,4096]{2,1,0:T(8,128)(2,1)}, u32[]{:S(2)}, u32[]{:S(2)}) async-start(bf16[8,120,4096]{2,1,0:T(8,128)(2,1)} %bitcast.83), calls=%async_computation | async-start | bytes 15728640 | tf_op jit(solution)/shard_map/all_to_all | solution.py:81
  87.9 1.6 collective-permute-start.3
  89.8 91.6 %psum.14 = f32[16,16]{1,0:T(8,128)S(1)} all-reduce(f32[16,16]{1,0:T(8,128)S(1)} %select_convert_fusion), channel_id=1, replica_groups=mesh['half'=2,'inner'=8,'dp'=2] {'inner'}, use_global_device_ids=true, to_apply=%region_4.5 | all-reduce | flops 256 | bytes 2048 | tf_op jit(solution)/shard_map/psum | solution.py:10
  181.5 6.1 %psum.15 = f32[16,16]{1,0:T(8,128)S(1)} all-reduce(f32[16,16]{1,0:T(8,128)S(1)} %psum.14), channel_id=1, replica_groups=mesh['half'=2,'inner'=8,'dp'=2] {'half'}, use_global_device_ids=true, to_apply=%region_5.6 | all-reduce | flops 256 | bytes 2048 | tf_op jit(solution)/shard_map/psum | solution.py:11
  190.0 6.9 %bitcast_select_fusion = bf16[1,960,4096]{2,1,0:T(8,128)(2,1)} fusion(pred[960]{0:T(1024)(128)(4,1)S(1)} %lt.80, bf16[1,960,4096]{2,1,0:T(8,128)(2,1)} %bitcast.81), kind=kLoop, calls=%fused_computation.8 | loop fusion | flops 3932160 | bytes 15729600 | tf_op jit(solution)/shard_map/jit(_where)/select_n | solution.py:91
  196.9 4.7 fusion.3
  201.6 3.3 fusion.6
  205.0 4.7 multiply_convert_fusion.2
  209.6 3.6 fusion.61
  213.2 5.3 %add_convert_fusion = bf16[960,2048]{1,0:T(8,128)(2,1)} fusion(f32[960,2048]{1,0:T(8,128)S(1)} %fusion.61, bf16[960,384]{1,0:T(8,128)(2,1)S(1)} %get-tuple-element.45, bf16[3,192,2048]{2,1,0:T(8,128)(2,1)S(1)} %constant_dynamic-update-slice_fusion.2, bf16[3,192,2048]{2,1,0:T(8,128)(2,1)} %collective-permute-done.3), kind=kOutput, calls=%fused_computation.9 | convolution fusion | flops 1517027328 | bytes 17252352 | tf_op jit(solution)/shard_map/erf,efd->erd/dot_general | solution.py:112
  218.5 5.1 %reshape.356 = bf16[1,8,2,60,2048]{4,3,2,1,0:T(8,128)(2,1)} reshape(bf16[960,2048]{1,0:T(8,128)(2,1)} %add_convert_fusion) | data formatting | bytes 7864320 | tf_op jit(solution)/shard_map/reshape | solution.py:120
  223.6 5.4 %convolution_convert_fusion = bf16[960,2048]{1,0:T(8,128)(2,1)} fusion(bf16[960,384]{1,0:T(8,128)(2,1)} %get-tuple-element.44, bf16[3,192,2048]{2,1,0:T(8,128)(2,1)} %collective-permute-done.3, bf16[3,192,2048]{2,1,0:T(8,128)(2,1)S(1)} %constant_dynamic-update-slice_fusion.2), kind=kOutput, calls=%fused_computation.25 | convolution fusion | flops 1515061248 | bytes 9388032 | tf_op jit(solution)/shard_map/erf,efd->erd/dot_general | solution.py:104
  229.0 4.9 %reshape.354 = bf16[1,8,2,60,2048]{4,3,2,1,0:T(8,128)(2,1)} reshape(bf16[960,2048]{1,0:T(8,128)(2,1)} %convolution_convert_fusion) | data formatting | bytes 7864320 | tf_op jit(solution)/shard_map/reshape | solution.py:119
  234.0 4.8 %fusion.64 = (bf16[1,8,1,60,2048]{4,3,2,1,0:T(8,128)(2,1)S(1)}, bf16[1,8,1,60,2048]{4,3,2,1,0:T(8,128)(2,1)S(1)}, bf16[1,8,1,60,2048]{4,3,2,1,0:T(8,128)(2,1)}, bf16[1,8,1,60,2048]{4,3,2,1,0:T(8,128)(2,1)S(1)}) fusion(bf16[1,8,2,60,2048]{4,3,2,1,0:T(8,128)(2,1)} %reshape.354, bf16[1,8,2,60,2048]{4,3,2,1,0:T(8,128)(2,1)} %reshape.356), kind=kLoop, calls=%fused_computation.140 | loop fusion | bytes 15728640 | tf_op jit(solution)/shard_map/slice | solution.py:123
  239.1 6.0 %copy.93 = bf16[8,2,60,2048]{3,1,2,0:T(2,128)(2,1)} copy(bf16[8,2,60,2048]{3,2,1,0:T(8,128)(2,1)S(1)} %maximum_bitcast_fusion.1) | data formatting | bytes 7864320 | tf_op jit(solution)/shard_map/reshape;transpose | solution.py:124
  245.2 4.5 all-to-all-start.2
  249.7 2.0 maximum_bitcast_fusion
  251.7 6.0 %copy.92 = bf16[8,2,60,2048]{3,1,2,0:T(2,128)(2,1)} copy(bf16[8,2,60,2048]{3,2,1,0:T(8,128)(2,1)S(1)} %maximum_bitcast_fusion) | data formatting | bytes 7864320 | tf_op jit(solution)/shard_map/reshape;transpose | solution.py:124
  257.7 37.3 %all-to-all-done.2 = bf16[8,2,60,2048]{3,1,2,0:T(2,128)(2,1)} async-done(((bf16[8,2,60,2048]{3,1,2,0:T(2,128)(2,1)}), bf16[8,2,60,2048]{3,1,2,0:T(2,128)(2,1)}, u32[]{:S(2)}, u32[]{:S(2)}) %all-to-all-start.2) | async-done | bytes 3932192 | tf_op jit(solution)/shard_map/all_to_all | solution.py:125
  295.0 4.9 %all-to-all-start.1 = ((bf16[8,2,60,2048]{3,1,2,0:T(2,128)(2,1)}), bf16[8,2,60,2048]{3,1,2,0:T(2,128)(2,1)}, u32[]{:S(2)}, u32[]{:S(2)}) async-start(bf16[8,2,60,2048]{3,1,2,0:T(2,128)(2,1)} %copy.92), calls=%async_computation.1 | async-start | bytes 7864320 | tf_op jit(solution)/shard_map/all_to_all | solution.py:125
  300.0 4.1 convolution_bitcast_fusion
  304.2 4.1 convolution_bitcast_fusion.1
  308.3 1.8 fusion.4
  311.7 1.6 collective-permute-start.6
  313.3 52.0 %collective-permute-done.6 = bf16[3,192,2048]{2,1,0:T(8,128)(2,1)S(1)} collective-permute-done((bf16[3,192,2048]{2,1,0:T(8,128)(2,1)S(1)}, bf16[3,192,2048]{2,1,0:T(8,128)(2,1)S(1)}, u32[]{:S(2)}, u32[]{:S(2)}) %collective-permute-start.6) | collective-permute-done | bytes 2359328 | tf_op jit(solution)/shard_map/ppermute | solution.py:15
  367.7 20.6 %slice_reduce_fusion.2 = (bf16[8,60,2048]{2,1,0:T(8,128)(2,1)}, bf16[8,60,2048]{2,1,0:T(8,128)(2,1)}) fusion(bf16[8,2,60,2048]{3,1,2,0:T(2,128)(2,1)} %all-to-all-done.2), kind=kLoop, calls=%fused_computation.21 | loop fusion | bytes 7864320 | tf_op jit(solution)/shard_map/slice | solution.py:141
  388.3 1.8 reshape_squeeze.13
  391.3 1.5 collective-permute-start.5
  392.8 20.7 %slice_reduce_fusion = (bf16[8,60,2048]{2,1,0:T(8,128)(2,1)}, bf16[8,60,2048]{2,1,0:T(8,128)(2,1)}) fusion(bf16[8,2,60,2048]{3,1,2,0:T(2,128)(2,1)} %all-to-all-done.1), kind=kLoop, calls=%fused_computation.19 | loop fusion | bytes 7864320 | tf_op jit(solution)/shard_map/slice | solution.py:142
  413.5 1.7 reshape_squeeze.12
  415.3 2.5 fusion.29
  418.0 2.7 reshape_squeeze.14
  420.8 2.1 convolution_convert_fusion.1
  426.7 2.7 fusion.23
  429.3 2.9 reshape_squeeze.15
  432.8 39.3 %collective-permute-done.4 = bf16[128,4096]{1,0:T(8,128)(2,1)} collective-permute-done((bf16[128,4096]{1,0:T(8,128)(2,1)}, bf16[128,4096]{1,0:T(8,128)(2,1)}, u32[]{:S(2)}, u32[]{:S(2)}) %collective-permute-start.4) | collective-permute-done | bytes 1048608 | tf_op jit(solution)/shard_map/ppermute | solution.py:15
  472.1 2.1 fusion.19
  474.2 2.3 add_convert_fusion.1
  (108 shorter events, 19.7 us)
Async XLA Ops:
  0.6 9.7 %copy-start.12 = (s32[128,6]{0,1:T(8,128)S(1)}, s32[128,6]{0,1:T(8,128)}, u32[]{:S(2)}) copy-start(s32[128,6]{0,1:T(8,128)} %param.10) | copy-start | bytes 9220
  0.6 9.8 %copy-start.11 = (f32[128,6]{0,1:T(8,128)S(1)}, f32[128,6]{0,1:T(8,128)}, u32[]{:S(2)}) copy-start(f32[128,6]{0,1:T(8,128)} %param.11) | copy-start | bytes 9220
  2.8 63.7 %collective-permute-start.1 = (bf16[128,4096]{1,0:T(8,128)(2,1)S(1)}, bf16[128,4096]{1,0:T(8,128)(2,1)S(1)}, u32[]{:S(2)}, u32[]{:S(2)}) collective-permute-start(bf16[128,4096]{1,0:T(8,128)(2,1)S(1)} %constant_dynamic-update-slice_fusion), channel_id=1, source_target_pairs={{0,16},{16,0},{1,17},{17,1},{2,18},{18,2},{3,19},{19,3},{4,20},{20... | collective-permute-start | bytes 3145736 | tf_op jit(solution)/shard_map/ppermute | solution.py:15
  10.3 42.5 %collective-permute-start = (s32[128,6]{0,1:T(8,128)S(1)}, s32[128,6]{0,1:T(8,128)S(1)}, u32[]{:S(2)}, u32[]{:S(2)}) collective-permute-start(s32[128,6]{0,1:T(8,128)S(1)} %multiply_add_fusion), channel_id=1, source_target_pairs={{0,16},{16,0},{1,17},{17,1},{2,18},{18,2},{3,19},{19,3},{4,20},{20... | collective-permute-start | bytes 9224 | tf_op jit(solution)/shard_map/ppermute | solution.py:15
  10.4 43.4 %collective-permute-start.2 = (f32[128,6]{0,1:T(8,128)S(1)}, f32[128,6]{0,1:T(8,128)S(1)}, u32[]{:S(2)}, u32[]{:S(2)}) collective-permute-start(f32[128,6]{0,1:T(8,128)S(1)} %copy-done.11), channel_id=1, source_target_pairs={{0,16},{16,0},{1,17},{17,1},{2,18},{18,2},{3,19},{19,3},{4,20},{20... | collective-permute-start | bytes 9224 | tf_op jit(solution)/shard_map/ppermute | solution.py:15
  66.6 2.3 copy-start.4
  81.3 5.1 %copy-start.7 = (bf16[1,192,2048]{2,1,0:T(8,128)(2,1)S(1)}, bf16[1,192,2048]{2,1,0:T(8,128)(2,1)}, u32[]{:S(2)}) copy-start(bf16[1,192,2048]{2,1,0:T(8,128)(2,1)} %param.13) | copy-start | bytes 2359300
  81.3 108.7 %all-to-all-start = ((bf16[8,120,4096]{2,1,0:T(8,128)(2,1)}), bf16[8,120,4096]{2,1,0:T(8,128)(2,1)}, u32[]{:S(2)}, u32[]{:S(2)}) async-start(bf16[8,120,4096]{2,1,0:T(8,128)(2,1)} %bitcast.83), calls=%async_computation | async-start | bytes 15728640 | tf_op jit(solution)/shard_map/all_to_all | solution.py:81
  86.4 1.4 copy-start.8
  86.4 102.1 %copy-start.13 = (s32[16]{0:T(128)S(1)}, s32[16]{0:T(128)}, u32[]{:S(2)}) copy-start(s32[16]{0:T(128)} %param.12) | copy-start | bytes 196
  87.9 109.1 %collective-permute-start.3 = (bf16[3,192,2048]{2,1,0:T(8,128)(2,1)S(1)}, bf16[3,192,2048]{2,1,0:T(8,128)(2,1)}, u32[]{:S(2)}, u32[]{:S(2)}) collective-permute-start(bf16[3,192,2048]{2,1,0:T(8,128)(2,1)S(1)} %constant_dynamic-update-slice_fusion.2), channel_id=1, source_target_pairs={{0,1},{1,0},{2,3},{3,2},{4,5},{5,4},{6,7},{7,6},{8,9},{9,8},{10,11... | collective-permute-start | bytes 7077896 | tf_op jit(solution)/shard_map/ppermute | solution.py:15
  196.9 4.7 copy-start.2
  209.6 3.6 copy-start.9
  245.2 49.9 %all-to-all-start.2 = ((bf16[8,2,60,2048]{3,1,2,0:T(2,128)(2,1)}), bf16[8,2,60,2048]{3,1,2,0:T(2,128)(2,1)}, u32[]{:S(2)}, u32[]{:S(2)}) async-start(bf16[8,2,60,2048]{3,1,2,0:T(2,128)(2,1)} %copy.93), calls=%async_computation.2 | async-start | bytes 7864320 | tf_op jit(solution)/shard_map/all_to_all | solution.py:125
  295.0 97.8 %all-to-all-start.1 = ((bf16[8,2,60,2048]{3,1,2,0:T(2,128)(2,1)}), bf16[8,2,60,2048]{3,1,2,0:T(2,128)(2,1)}, u32[]{:S(2)}, u32[]{:S(2)}) async-start(bf16[8,2,60,2048]{3,1,2,0:T(2,128)(2,1)} %copy.92), calls=%async_computation.1 | async-start | bytes 7864320 | tf_op jit(solution)/shard_map/all_to_all | solution.py:125
  300.0 4.1 copy-start.10
  300.0 8.3 %slice-start = ((s8[7864320]{0:T(1024)(128)(4,1)}), s8[4194304]{0:T(1024)(128)(4,1)S(1)}, s32[]{:S(2)}) async-start(s8[7864320]{0:T(1024)(128)(4,1)} %bitcast.84), calls=%async_computation.3 | async-start | bytes 8388608
  304.1 4.2 slice-start.1
  304.1 4.2 copy-start.14
  311.7 53.7 %collective-permute-start.6 = (bf16[3,192,2048]{2,1,0:T(8,128)(2,1)S(1)}, bf16[3,192,2048]{2,1,0:T(8,128)(2,1)S(1)}, u32[]{:S(2)}, u32[]{:S(2)}) collective-permute-start(bf16[3,192,2048]{2,1,0:T(8,128)(2,1)S(1)} %slice.257), channel_id=1, source_target_pairs={{0,1},{1,0},{2,3},{3,2},{4,5},{5,4},{6,7},{7,6},{8,9},{9,8},{10,11... | collective-permute-start | bytes 7077896 | tf_op jit(solution)/shard_map/ppermute | solution.py:15
  388.3 1.9 copy-start.5
  390.1 23.4 %copy-start = (bf16[480,2048]{1,0:T(8,128)(2,1)}, bf16[480,2048]{1,0:T(8,128)(2,1)S(1)}, u32[]{:S(2)}) copy-start(bf16[480,2048]{1,0:T(8,128)(2,1)S(1)} %reshape_squeeze.13) | copy-start | bytes 5898244
  391.3 41.0 %collective-permute-start.5 = (f32[128,6]{0,1:T(8,128)S(1)}, f32[128,6]{0,1:T(8,128)S(1)}, u32[]{:S(2)}, u32[]{:S(2)}) collective-permute-start(f32[128,6]{0,1:T(8,128)S(1)} %get-tuple-element.32), channel_id=1, source_target_pairs={{0,16},{16,0},{1,17},{17,1},{2,18},{18,2},{3,19},{19,3},{4,20},{20... | collective-permute-start | bytes 9224 | tf_op jit(solution)/shard_map/ppermute | solution.py:15
  420.8 4.7 copy-start.6
  424.0 48.1 %collective-permute-start.4 = (bf16[128,4096]{1,0:T(8,128)(2,1)}, bf16[128,4096]{1,0:T(8,128)(2,1)}, u32[]{:S(2)}, u32[]{:S(2)}) collective-permute-start(bf16[128,4096]{1,0:T(8,128)(2,1)} %pad_maximum_fusion.3), channel_id=1, source_target_pairs={{0,16},{16,0},{1,17},{17,1},{2,18},{18,2},{3,19},{19,3},{4,20},{20... | collective-permute-start | bytes 3145736 | tf_op jit(solution)/shard_map/ppermute | solution.py:15
  429.3 42.8 %copy-start.1 = (f32[384,2048]{1,0:T(8,128)S(1)}, f32[384,2048]{1,0:T(8,128)}, u32[]{:S(2)}) copy-start(f32[384,2048]{1,0:T(8,128)} %fusion.23) | copy-start | bytes 9437188
  432.2 42.0 %copy-start.3 = (bf16[480,2048]{1,0:T(8,128)(2,1)S(1)}, bf16[480,2048]{1,0:T(8,128)(2,1)}, u32[]{:S(2)}) copy-start(bf16[480,2048]{1,0:T(8,128)(2,1)} %reshape_squeeze.15) | copy-start | bytes 5898244
